TPU v7x, 256 devices: a whole 4x4x8 slice. The times are simulated.
256 devices in a mesh: ctx: 16 (over z, core), ch: 16 (over y, x).
Axes of the slice: x: 4, y: 4, z: 8, core: 2. Of those that a mesh axis runs over, the one named last changes fastest.
Arguments:
- inputs: bfloat16 [4096, 4096], P('ctx', 'ch'), may hold values from -6 to 6
- gating: bfloat16 [4096, 4096], P('ctx', 'ch'), may hold values from -6 to 6
- filter_taps: bfloat16 [4096, 4096], P('ctx', 'ch'), may hold values from -2.25 to 2.25
- skip_gain: float32 [4096], P('ch'), may hold values from 0.5 to 1.5
- w_out: bfloat16 [4096, 4096], P('ch'), may hold values from -0.09375 to 0.09375
- cotangent: bfloat16 [4096, 4096], P('ctx', 'ch'), may hold values from -0.3125 to 0.3125
Outputs:
- output: bfloat16 [4096, 4096], P('ctx', 'ch')
- filter_grad: float32 [4096, 4096], P('ctx', 'ch')
All inputs are finite; a program needn't handle non-finite values.
Results may differ from a plain program's by a relative error of at most 0.015.
Values may be sent and summed in bfloat16 or wider, within the bound.
No kernel may reach another device: no remote copies, remote signals or barrier semaphores. Data moves between devices by JAX's collectives and lax.ppermute only.
A program may use at most 64 MiB of HBM per device.

v0:
```python
import math
import jax
import jax.numpy as jnp
from jax import lax
from jax.sharding import PartitionSpec as P

exact_prec = lax.Precision.HIGHEST


def spectral_tables(block_len):
    time_ids = jnp.arange(2 * block_len, dtype=jnp.int32)
    freq_ids = jnp.arange(block_len, dtype=jnp.int32)
    phase_ids = freq_ids[:, None] * time_ids[None, :] % (2 * block_len)
    angles = phase_ids.astype(jnp.float32) * (math.pi / block_len)
    parity = jnp.where(time_ids % 2 == 0, 1.0, -1.0).astype(jnp.float32)[None, :]
    is_first = (freq_ids == 0)[:, None]
    forward = jnp.concatenate(
        [jnp.cos(angles), jnp.where(is_first, parity, -jnp.sin(angles))], axis=0
    )
    norm_scale = 1.0 / (2 * block_len)
    real_rows = jnp.where(is_first, 1.0, 2.0) * jnp.cos(angles) * norm_scale
    imag_rows = jnp.where(is_first, parity, -2.0 * jnp.sin(angles)) * norm_scale
    inverse = jnp.concatenate([real_rows, imag_rows], axis=0).T
    first_bin = is_first.astype(jnp.float32)
    return (forward, inverse, first_bin)


def spec_product(first_spec, second_spec, first_bin):
    bin_count = first_bin.shape[0]
    first_real, first_imag = (first_spec[..., :bin_count, :], first_spec[..., bin_count:, :])
    second_real, second_imag = (second_spec[..., :bin_count, :], second_spec[..., bin_count:, :])
    others = 1.0 - first_bin
    real_part = first_real * second_real - others * first_imag * second_imag
    imag_part = (
        others * (first_real * second_imag + first_imag * second_real)
        + first_bin * first_imag * second_imag
    )
    return jnp.concatenate([real_part, imag_part], axis=-2)


def conj_product(first_spec, second_spec, first_bin):
    bin_count = first_bin.shape[0]
    first_real, first_imag = (first_spec[..., :bin_count, :], first_spec[..., bin_count:, :])
    second_real, second_imag = (second_spec[..., :bin_count, :], second_spec[..., bin_count:, :])
    others = 1.0 - first_bin
    real_part = first_real * second_real + others * first_imag * second_imag
    imag_part = (
        others * (first_imag * second_real - first_real * second_imag)
        + first_bin * first_imag * second_imag
    )
    return jnp.concatenate([real_part, imag_part], axis=-2)


def transform(dft_table, block_rows):
    return jnp.dot(dft_table, block_rows.astype(jnp.float32), precision=exact_prec)


def body(inputs, gating, filter_taps, skip_gain, w_out, cotangent):
    block_len, channels = inputs.shape
    ctx_count = lax.axis_size("ctx")
    position = lax.axis_index("ctx")
    forward, inverse, first_bin = spectral_tables(block_len)
    first_half = forward[:, :block_len]
    second_half = forward[:, block_len:]
    upstream = lax.dot_general(
        lax.all_gather(cotangent, "ch", axis=1, tiled=True),
        w_out,
        (((1,), (1,)), ((), ())),
        preferred_element_type=jnp.float32,
    )
    gate_wide = gating.astype(jnp.float32)
    grad_mixed = upstream * gate_wide
    signal_all, kernel_all = (
        lax.all_gather(inputs, "ctx", axis=0, tiled=True),
        lax.all_gather(filter_taps, "ctx", axis=0, tiled=True),
    )
    padded = jnp.concatenate(
        [jnp.zeros((block_len, channels), signal_all.dtype), signal_all], axis=0
    )
    own_spec = transform(second_half, grad_mixed)

    def lag_step(lag_index, state_pair):
        running, term_table = state_pair
        segment = lax.dynamic_slice_in_dim(
            padded, (position - lag_index) * block_len, 2 * block_len, 0
        )
        seg_spec = transform(forward, segment)
        kernel_block = lax.dynamic_slice_in_dim(kernel_all, lag_index * block_len, block_len, 0)
        running = running + spec_product(transform(first_half, kernel_block), seg_spec, first_bin)
        term_table = lax.dynamic_update_index_in_dim(
            term_table, conj_product(own_spec, seg_spec, first_bin), lag_index, 0
        )
        return (running, term_table)

    start_terms = jnp.zeros((ctx_count, 2 * block_len, channels), jnp.float32)
    start_spec = jnp.zeros((2 * block_len, channels), jnp.float32)
    running, term_table = lax.fori_loop(0, position + 1, lag_step, (start_spec, start_terms))
    convolved = jnp.dot(inverse[block_len:], running, precision=exact_prec)
    convolved, term_table = (convolved, term_table)
    summed = lax.psum_scatter(
        term_table.astype(jnp.bfloat16), "ctx", scatter_dimension=0, tiled=True
    ).astype(jnp.float32)
    filter_grad = jnp.dot(inverse[:block_len], summed[0], precision=exact_prec)
    mixed_sum = convolved + skip_gain[None, :] * inputs.astype(jnp.float32)
    gated_rows = (gate_wide * mixed_sum).astype(jnp.bfloat16)
    partial_out = jnp.dot(gated_rows, w_out, preferred_element_type=jnp.float32)
    output = lax.psum_scatter(
        partial_out.astype(jnp.bfloat16), "ch", scatter_dimension=1, tiled=True
    )
    return (output, filter_grad)


def solution(mesh):
    return jax.shard_map(
        body,
        mesh=mesh,
        in_specs=(
            P("ctx", "ch"),
            P("ctx", "ch"),
            P("ctx", "ch"),
            P("ch"),
            P("ch", None),
            P("ctx", "ch"),
        ),
        out_specs=(P("ctx", "ch"), P("ctx", "ch")),
        check_vma=False,
    )
```

profile of v0, /device:TPU:2, one launch (start us, length us, event | category | flops | bytes accessed | tf_op | source)
XLA Modules:
  0.0 419.1 jit_solution(11839190690769091835)
XLA Ops:
  9.5 1.9 fusion.24
  11.4 2.8 select_multiply_fusion
  14.2 0.9 fusion.12
  15.0 1.1 pad_maximum_fusion
  16.2 36.1 %all-gather.6.cloned.1.call-done = bf16[4096,256]{1,0:T(8,128)(2,1)} async-done(((bf16[256,256]{1,0:T(8,128)(2,1)}), bf16[4096,256]{1,0:T(8,128)(2,1)}) %all-gather.6.cloned.1.call-update) | async-done | bytes 2097168 | tf_op jit(solution)/shard_map/all_gather | solution.py:74
  52.2 3.1 concatenate.17
  55.4 49.4 %all-gather.8.cloned.1.call-done = bf16[256,4096]{1,0:T(8,128)(2,1)} async-done(((bf16[256,256]{1,0:T(8,128)(2,1)}), bf16[256,4096]{1,0:T(8,128)(2,1)}) %all-gather.8.cloned.1.call-update) | async-done | bytes 2097168 | tf_op jit(solution)/shard_map/all_gather | solution.py:66
  104.8 2.3 convolution_multiply_fusion
  107.1 1.5 fusion.14
  108.6 37.2 %all-gather.4.cloned.1.call-done = bf16[4096,256]{1,0:T(8,128)(2,1)} async-done(((bf16[256,256]{1,0:T(8,128)(2,1)}), bf16[4096,256]{1,0:T(8,128)(2,1)}) %all-gather.4.cloned.1.call-update) | async-done | bytes 2097168 | tf_op jit(solution)/shard_map/all_gather | solution.py:75
  145.8 0.8 broadcast_in_dim.64
  146.6 2.3 broadcast_in_dim.65
  149.0 7.6 %while.14 = (s32[]{:T(128)}, f32[512,256]{0,1:T(8,128)}, bf16[16,512,256]{1,2,0:T(8,128)(2,1)}, s32[]{:T(128)}, bf16[4096,256]{1,0:T(8,128)(2,1)}, /*index=5*/f3...) while((s32[]{:T(128)}, f32[512,256]{0,1:T(8,128)}, ...), condition=%wide.region_1.2_spmd.clone.clone, body=%wide.region_0.1_spmd.clone.clone.sunk | while | flops 1210319616 | bytes 8002867 | solution.py:97
  149.0 1.6 convolution_bitcast_fusion.4
  150.6 2.1 convolution_bitcast_fusion.5
  152.8 1.9 maximum_add_fusion.2
  154.7 1.1 multiply_add_fusion.4
  156.7 2.0 multiply_multiply_fusion
  158.7 1.0 copy-done.2
  159.7 1.0 fusion.8
  160.7 2.1 convolution_convert_fusion
  162.8 167.4 %reduce-scatter.5.cloned.1.call-done = bf16[1,512,256]{1,2,0:T(8,128)(2,1)} async-done(((bf16[16,512,256]{1,2,0:T(8,128)(2,1)}), bf16[1,512,256]{1,2,0:T(8,128)(2,1)}) %reduce-scatter.5.cloned.1.call-update) | async-done | bytes 262160 | tf_op jit(solution)/shard_map/reduce_scatter | solution.py:100
  330.2 2.2 fusion.16
  332.5 80.1 %reduce-scatter.3.cloned.1.call-done = bf16[256,256]{1,0:T(8,128)(2,1)} async-done(((bf16[256,4096]{1,0:T(8,128)(2,1)}), bf16[256,256]{1,0:T(8,128)(2,1)}) %reduce-scatter.3.cloned.1.call-update) | async-done | bytes 131088 | tf_op jit(solution)/shard_map/reduce_scatter | solution.py:107
  (33 shorter events, 3.2 us)
Async XLA Ops:
  7.2 97.6 %copy-start = (bf16[256,4096]{1,0:T(8,128)(2,1)S(1)}, bf16[256,4096]{1,0:T(8,128)(2,1)}, u32[]{:S(2)}) copy-start(bf16[256,4096]{1,0:T(8,128)(2,1)} %param.12) | copy-start | bytes 6291460
  7.2 45.1 %all-gather.6.cloned.1.call-start = ((), (), s32[]{:S(2)}) async-start(), calls=%async_computation.3 | async-start | bytes 2228224 | tf_op jit(solution)/shard_map/all_gather | solution.py:74
  7.9 96.8 %all-gather.8.cloned.1.call-start = ((), (), s32[]{:S(2)}) async-start(), calls=%async_computation.4 | async-start | bytes 2228224 | tf_op jit(solution)/shard_map/all_gather | solution.py:66
  8.7 137.1 %all-gather.4.cloned.1.call-start = ((), (), s32[]{:S(2)}) async-start(), calls=%async_computation.2 | async-start | bytes 2228224 | tf_op jit(solution)/shard_map/all_gather | solution.py:75
  9.4 320.8 %reduce-scatter.5.cloned.1.call-start = ((), (), s32[]{:S(2)}) async-start(), calls=%async_computation.6 | async-start | bytes 4456448 | tf_op jit(solution)/shard_map/reduce_scatter | solution.py:100
  16.2 88.6 %copy-start.5 = (bf16[256,256]{1,0:T(8,128)(2,1)S(1)}, bf16[256,256]{1,0:T(8,128)(2,1)}, u32[]{:S(2)}) copy-start(bf16[256,256]{1,0:T(8,128)(2,1)} %param.9) | copy-start | bytes 393220
  156.5 2.1 copy-start.4
  156.6 3.1 copy-start.1
  156.6 3.1 copy-start.6
  156.6 3.1 copy-start.7
  156.6 256.0 %reduce-scatter.3.cloned.1.call-start = ((), (), s32[]{:S(2)}) async-start(), calls=%async_computation.5 | async-start | bytes 2228224 | tf_op jit(solution)/shard_map/reduce_scatter | solution.py:107
  158.7 1.0 copy-start.2
  162.8 167.5 %copy-start.3 = (f32[512,512]{0,1:T(8,128)S(1)}, f32[512,512]{0,1:T(8,128)}, u32[]{:S(2)}) copy-start(f32[512,512]{0,1:T(8,128)} %copy-done.2) | copy-start | bytes 3145732
Sparse Core Ops, SparseCore 0:
  9.8 42.3 all-gather.5
  54.6 50.0 all-gather.7
  106.6 39.1 all-gather.3
  156.7 173.5 reduce-scatter.4
  334.2 78.3 reduce-scatter.2
where the time goes:
time: 421 us; the launch traced here: 419 us
  waiting for transfers between devices  372 us (88%)
  between operations  13.9 us (3%)
  matrix products  12.8 us (3%)
  other arithmetic  12.6 us (3%)
  local copies, waits for them, and re-layouts  7.34 us (2%)
    reduce_scatter x1, waiting for transfers between devices, body(): lax.psum_scatter(term_table.astype(jnp.bfloat16), 'ctx', scatter_dimensio...  167 us
    reduce_scatter x1, waiting for transfers between devices, body(): lax.psum_scatter(partial_out.astype(jnp.bfloat16), 'ch', scatter_dimensio...  80.1 us
    all_gather x1, waiting for transfers between devices, body(): lax.all_gather(cotangent, 'ch', axis=1, tiled=True)  49.4 us
    all_gather x1, waiting for transfers between devices, body(): lax.all_gather(filter_taps, 'ctx', axis=0, tiled=True)  37.2 us
    all_gather x1, waiting for transfers between devices, body(): lax.all_gather(inputs, 'ctx', axis=0, tiled=True)  36.1 us
  transfers between devices with their start and end apart: 5, of which 5 were waited for; matrix products, arithmetic and copies ran while one was open for 5% of the time, Pallas kernels for 0%

commit v1 on v0

--- a/solution.py
+++ b/solution.py
@@ -5,6 +5,33 @@
 from jax.sharding import PartitionSpec as P
 
 exact_prec = lax.Precision.HIGHEST
+
+
+def wait_case_here(incoming_x):
+    width = lax.axis_size("ctx")
+    by_place = []
+    kk = 0
+    while kk < width:
+        by_place.append((kk, (kk + 1) % width))
+        kk += 1
+    log = []
+    kk = 0
+    while kk < width:
+        log.append((kk, (kk - 1) % width))
+        kk += 1
+    r2, front = ([incoming_x], [incoming_x])
+    for _ in range(width // 2):
+        o_now = lax.ppermute(r2[-1], "ctx", by_place)
+        r2.append(o_now)
+    pp = 0
+    while pp < (width - 1) // 2:
+        value_now = lax.ppermute(front[-1], "ctx", perm=log)
+        front.append(value_now)
+        pp = pp + 1
+    low = jnp.concatenate([*r2[::-1], *front[1:]], 0)
+    mat_out = lax.axis_index("ctx")
+    spare = jnp.roll(low, (mat_out - width // 2) * incoming_x.shape[0], axis=0)
+    return spare
 
 
 def spectral_tables(block_len):
@@ -72,7 +99,7 @@
     grad_mixed = upstream * gate_wide
     signal_all, kernel_all = (
         lax.all_gather(inputs, "ctx", axis=0, tiled=True),
-        lax.all_gather(filter_taps, "ctx", axis=0, tiled=True),
+        wait_case_here(filter_taps),
     )
     padded = jnp.concatenate(
         [jnp.zeros((block_len, channels), signal_all.dtype), signal_all], axis=0

time: 421 us -> 385 us (0.914)
  waiting for transfers between devices: 372 us -> 300 us
  starting transfers between devices: 0.19 us -> 21.6 us
  local copies, waits for them, and re-layouts: 7.34 us -> 22 us
    all_gather x1, waiting for transfers between devices: 49.4 us -> 0.01 us  [body(): lax.all_gather(cotangent, 'ch', axis=1, tiled=True)]
    all_gather x1 -> x0, waiting for transfers between devices: 37.2 us -> none  [body(): lax.all_gather(filter_taps, 'ctx', axis=0, tiled=True)]
    ppermute x0 -> x15, waiting for transfers between devices: none -> 21.8 us  [the longest x8 20.5 us: wait_case_here(): o_now = lax.ppermute(r2[-1], 'ctx', by_place)]
    ppermute x0 -> x15, starting transfers between devices: none -> 21.3 us  [the longest x7 21.2 us: wait_case_here(): value_now = lax.ppermute(front[-1], 'ctx', perm=log)]
    unnamed x16 -> x83, local copies, waits for them, and re-layouts: 1.01 us -> 14.1 us
    all_gather x1, waiting for transfers between devices: 36.1 us -> 29.6 us  [body(): lax.all_gather(inputs, 'ctx', axis=0, tiled=True)]
  transfers between devices with their start and end apart: 5 -> 19, of which waited for: 5 -> 13; matrix products, arithmetic and copies ran while one was open for 5% -> 8% of each run, Pallas kernels for 0% -> 0%
where the time goes in v1:
time: 385 us; the launch traced here: 383 us
  waiting for transfers between devices  300 us (78%)
  local copies, waits for them, and re-layouts  22 us (6%)
  starting transfers between devices  21.6 us (6%)
  between operations  14.3 us (4%)
  matrix products  12.8 us (3%)
  other arithmetic  12.5 us (3%)
    reduce_scatter x1, waiting for transfers between devices, body(): lax.psum_scatter(term_table.astype(jnp.bfloat16), 'ctx', scatter_dimensio...  168 us
    reduce_scatter x1, waiting for transfers between devices, body(): lax.psum_scatter(partial_out.astype(jnp.bfloat16), 'ch', scatter_dimensio...  80.2 us
    all_gather x1, waiting for transfers between devices, body(): lax.all_gather(inputs, 'ctx', axis=0, tiled=True)  29.6 us
    ppermute x7, starting transfers between devices, wait_case_here(): value_now = lax.ppermute(front[-1], 'ctx', perm=log)  21.2 us
    ppermute x8, waiting for transfers between devices, wait_case_here(): o_now = lax.ppermute(r2[-1], 'ctx', by_place)  20.5 us
    unnamed x83, local copies, waits for them, and re-layouts  14.1 us
  transfers between devices with their start and end apart: 19, of which 13 were waited for; matrix products, arithmetic and copies ran while one was open for 8% of the time, Pallas kernels for 0%

profile of v1, /device:TPU:2, one launch (start us, length us, event | category | flops | bytes accessed | tf_op | source)
XLA Modules:
  0.0 383.1 jit_solution(9141744302719295832)
XLA Ops:
  8.0 8.1 %collective-permute-done = bf16[256,256]{1,0:T(8,128)(2,1)S(1)} collective-permute-done((bf16[256,256]{1,0:T(8,128)(2,1)}, bf16[256,256]{1,0:T(8,128)(2,1)S(1)}, u32[]{:S(2)}, u32[]{:S(2)}) %collective-permute-start) | collective-permute-done | bytes 131104 | tf_op jit(solution)/shard_map/ppermute | solution.py:24
  16.1 3.0 collective-permute-start.8
  19.1 2.6 collective-permute-done.1
  21.9 3.0 collective-permute-start.9
  24.9 2.4 collective-permute-done.2
  27.4 3.1 collective-permute-start.10
  30.5 2.4 collective-permute-done.3
  33.1 3.1 collective-permute-start.11
  36.1 2.4 collective-permute-done.4
  38.7 3.1 collective-permute-start.12
  41.7 2.4 collective-permute-done.5
  44.2 2.8 select_multiply_fusion
  49.0 2.9 collective-permute-start.13
  54.7 3.1 collective-permute-start.14
  72.7 2.3 convolution_multiply_fusion
  76.5 29.6 %all-gather.3.cloned.1.call-done = bf16[4096,256]{1,0:T(8,128)(2,1)} async-done(((bf16[256,256]{1,0:T(8,128)(2,1)}), bf16[4096,256]{1,0:T(8,128)(2,1)}) %all-gather.3.cloned.1.call-update) | async-done | bytes 2097168 | tf_op jit(solution)/shard_map/all_gather | solution.py:101
  106.1 3.1 concatenate.24
  110.1 2.4 broadcast_in_dim.65
  112.5 7.6 %while.14 = (s32[]{:T(128)}, f32[512,256]{0,1:T(8,128)}, bf16[16,512,256]{1,2,0:T(8,128)(2,1)}, s32[]{:T(128)}, bf16[4096,256]{1,0:T(8,128)(2,1)}, /*index=5*/f3...) while((s32[]{:T(128)}, f32[512,256]{0,1:T(8,128)}, ...), condition=%wide.region_1.2_spmd.clone.clone, body=%wide.region_0.1_spmd.clone.clone.sunk | while | flops 1210319616 | bytes 8002867 | solution.py:124
  114.1 2.1 convolution_bitcast_fusion.5
  124.4 2.1 convolution_convert_fusion
  126.5 167.7 %reduce-scatter.5.cloned.1.call-done = bf16[1,512,256]{1,2,0:T(8,128)(2,1)} async-done(((bf16[16,512,256]{1,2,0:T(8,128)(2,1)}), bf16[1,512,256]{1,2,0:T(8,128)(2,1)}) %reduce-scatter.5.cloned.1.call-update) | async-done | bytes 262160 | tf_op jit(solution)/shard_map/reduce_scatter | solution.py:127
  294.2 2.2 fusion.16
  296.4 80.2 %reduce-scatter.3.cloned.1.call-done = bf16[256,256]{1,0:T(8,128)(2,1)} async-done(((bf16[256,4096]{1,0:T(8,128)(2,1)}), bf16[256,256]{1,0:T(8,128)(2,1)}) %reduce-scatter.3.cloned.1.call-update) | async-done | bytes 131088 | tf_op jit(solution)/shard_map/reduce_scatter | solution.py:134
  (129 shorter events, 32.6 us)
Async XLA Ops:
  7.2 65.6 %copy-start = (bf16[256,4096]{1,0:T(8,128)(2,1)S(1)}, bf16[256,4096]{1,0:T(8,128)(2,1)}, u32[]{:S(2)}) copy-start(bf16[256,4096]{1,0:T(8,128)(2,1)} %param.12) | copy-start | bytes 6291460
  7.2 57.1 %copy-start.7 = (bf16[256,256]{1,0:T(8,128)(2,1)S(1)}, bf16[256,256]{1,0:T(8,128)(2,1)}, u32[]{:S(2)}) copy-start(bf16[256,256]{1,0:T(8,128)(2,1)} %param.10) | copy-start | bytes 393220
  7.2 65.5 %all-gather.5.cloned.1.call-start = ((), (), s32[]{:S(2)}) async-start(), calls=%async_computation.3 | async-start | bytes 2228224 | tf_op jit(solution)/shard_map/all_gather | solution.py:93
  7.9 98.2 %all-gather.3.cloned.1.call-start = ((), (), s32[]{:S(2)}) async-start(), calls=%async_computation.2 | async-start | bytes 2228224 | tf_op jit(solution)/shard_map/all_gather | solution.py:101
  8.0 8.2 %collective-permute-start = (bf16[256,256]{1,0:T(8,128)(2,1)}, bf16[256,256]{1,0:T(8,128)(2,1)S(1)}, u32[]{:S(2)}, u32[]{:S(2)}) collective-permute-start(bf16[256,256]{1,0:T(8,128)(2,1)} %param.10), channel_id=1, source_target_pairs={{0,16},{16,32},{32,48},{48,64},{64,80},{80,96},{96,112},{112,128},... | collective-permute-start | bytes 393224 | tf_op jit(solution)/shard_map/ppermute | solution.py:24
  16.1 5.6 %collective-permute-start.1 = (bf16[256,256]{1,0:T(8,128)(2,1)S(1)}, bf16[256,256]{1,0:T(8,128)(2,1)S(1)}, u32[]{:S(2)}, u32[]{:S(2)}) collective-permute-start(bf16[256,256]{1,0:T(8,128)(2,1)S(1)} %collective-permute-done), channel_id=1, source_target_pairs={{0,16},{16,32},{32,48},{48,64},{64,80},{80,96},{96,112},{112,128},... | collective-permute-start | bytes 393224 | tf_op jit(solution)/shard_map/ppermute | solution.py:24
  16.1 5.8 %collective-permute-start.8 = (bf16[256,256]{1,0:T(8,128)(2,1)}, bf16[256,256]{1,0:T(8,128)(2,1)S(1)}, u32[]{:S(2)}, u32[]{:S(2)}) collective-permute-start(bf16[256,256]{1,0:T(8,128)(2,1)} %param.10), channel_id=1, source_target_pairs={{0,240},{16,0},{32,16},{48,32},{64,48},{80,64},{96,80},{112,96},{1... | collective-permute-start | bytes 393224 | tf_op jit(solution)/shard_map/ppermute | solution.py:28
  21.7 5.6 %collective-permute-start.2 = (bf16[256,256]{1,0:T(8,128)(2,1)S(1)}, bf16[256,256]{1,0:T(8,128)(2,1)S(1)}, u32[]{:S(2)}, u32[]{:S(2)}) collective-permute-start(bf16[256,256]{1,0:T(8,128)(2,1)S(1)} %collective-permute-done.1), channel_id=1, source_target_pairs={{0,16},{16,32},{32,48},{48,64},{64,80},{80,96},{96,112},{112,128},... | collective-permute-start | bytes 393224 | tf_op jit(solution)/shard_map/ppermute | solution.py:24
  21.9 42.5 %copy-start.8 = (bf16[256,256]{1,0:T(8,128)(2,1)}, bf16[256,256]{1,0:T(8,128)(2,1)S(1)}, u32[]{:S(2)}) copy-start(bf16[256,256]{1,0:T(8,128)(2,1)S(1)} %collective-permute-done.8) | copy-start | bytes 393220
  21.9 5.5 %collective-permute-start.9 = (bf16[256,256]{1,0:T(8,128)(2,1)S(1)}, bf16[256,256]{1,0:T(8,128)(2,1)S(1)}, u32[]{:S(2)}, u32[]{:S(2)}) collective-permute-start(bf16[256,256]{1,0:T(8,128)(2,1)S(1)} %collective-permute-done.8), channel_id=1, source_target_pairs={{0,240},{16,0},{32,16},{48,32},{64,48},{80,64},{96,80},{112,96},{1... | collective-permute-start | bytes 393224 | tf_op jit(solution)/shard_map/ppermute | solution.py:28
  27.4 16.8 %copy-start.13 = (bf16[256,256]{1,0:T(8,128)(2,1)}, bf16[256,256]{1,0:T(8,128)(2,1)S(1)}, u32[]{:S(2)}) copy-start(bf16[256,256]{1,0:T(8,128)(2,1)S(1)} %collective-permute-done.2) | copy-start | bytes 393220
  27.4 5.6 %collective-permute-start.3 = (bf16[256,256]{1,0:T(8,128)(2,1)S(1)}, bf16[256,256]{1,0:T(8,128)(2,1)S(1)}, u32[]{:S(2)}, u32[]{:S(2)}) collective-permute-start(bf16[256,256]{1,0:T(8,128)(2,1)S(1)} %collective-permute-done.2), channel_id=1, source_target_pairs={{0,16},{16,32},{32,48},{48,64},{64,80},{80,96},{96,112},{112,128},... | collective-permute-start | bytes 393224 | tf_op jit(solution)/shard_map/ppermute | solution.py:24
  27.4 5.6 %collective-permute-start.10 = (bf16[256,256]{1,0:T(8,128)(2,1)S(1)}, bf16[256,256]{1,0:T(8,128)(2,1)S(1)}, u32[]{:S(2)}, u32[]{:S(2)}) collective-permute-start(bf16[256,256]{1,0:T(8,128)(2,1)S(1)} %collective-permute-done.9), channel_id=1, source_target_pairs={{0,240},{16,0},{32,16},{48,32},{64,48},{80,64},{96,80},{112,96},{1... | collective-permute-start | bytes 393224 | tf_op jit(solution)/shard_map/ppermute | solution.py:28
  33.0 5.6 %collective-permute-start.4 = (bf16[256,256]{1,0:T(8,128)(2,1)S(1)}, bf16[256,256]{1,0:T(8,128)(2,1)S(1)}, u32[]{:S(2)}, u32[]{:S(2)}) collective-permute-start(bf16[256,256]{1,0:T(8,128)(2,1)S(1)} %collective-permute-done.3), channel_id=1, source_target_pairs={{0,16},{16,32},{32,48},{48,64},{64,80},{80,96},{96,112},{112,128},... | collective-permute-start | bytes 393224 | tf_op jit(solution)/shard_map/ppermute | solution.py:24
  33.0 261.2 %reduce-scatter.5.cloned.1.call-start = ((), (), s32[]{:S(2)}) async-start(), calls=%async_computation.5 | async-start | bytes 4456448 | tf_op jit(solution)/shard_map/reduce_scatter | solution.py:127
  33.1 5.6 %collective-permute-start.11 = (bf16[256,256]{1,0:T(8,128)(2,1)S(1)}, bf16[256,256]{1,0:T(8,128)(2,1)S(1)}, u32[]{:S(2)}, u32[]{:S(2)}) collective-permute-start(bf16[256,256]{1,0:T(8,128)(2,1)S(1)} %collective-permute-done.10), channel_id=1, source_target_pairs={{0,240},{16,0},{32,16},{48,32},{64,48},{80,64},{96,80},{112,96},{1... | collective-permute-start | bytes 393224 | tf_op jit(solution)/shard_map/ppermute | solution.py:28
  38.6 5.6 %collective-permute-start.5 = (bf16[256,256]{1,0:T(8,128)(2,1)S(1)}, bf16[256,256]{1,0:T(8,128)(2,1)S(1)}, u32[]{:S(2)}, u32[]{:S(2)}) collective-permute-start(bf16[256,256]{1,0:T(8,128)(2,1)S(1)} %collective-permute-done.4), channel_id=1, source_target_pairs={{0,16},{16,32},{32,48},{48,64},{64,80},{80,96},{96,112},{112,128},... | collective-permute-start | bytes 393224 | tf_op jit(solution)/shard_map/ppermute | solution.py:24
  38.7 10.3 %collective-permute-start.12 = (bf16[256,256]{1,0:T(8,128)(2,1)S(1)}, bf16[256,256]{1,0:T(8,128)(2,1)}, u32[]{:S(2)}, u32[]{:S(2)}) collective-permute-start(bf16[256,256]{1,0:T(8,128)(2,1)S(1)} %collective-permute-done.11), channel_id=1, source_target_pairs={{0,240},{16,0},{32,16},{48,32},{64,48},{80,64},{96,80},{112,96},{1... | collective-permute-start | bytes 393224 | tf_op jit(solution)/shard_map/ppermute | solution.py:28
  44.2 7.7 %collective-permute-start.6 = (bf16[256,256]{1,0:T(8,128)(2,1)S(1)}, bf16[256,256]{1,0:T(8,128)(2,1)}, u32[]{:S(2)}, u32[]{:S(2)}) collective-permute-start(bf16[256,256]{1,0:T(8,128)(2,1)S(1)} %collective-permute-done.5), channel_id=1, source_target_pairs={{0,16},{16,32},{32,48},{48,64},{64,80},{80,96},{96,112},{112,128},... | collective-permute-start | bytes 393224 | tf_op jit(solution)/shard_map/ppermute | solution.py:24
  49.0 5.8 %collective-permute-start.13 = (bf16[256,256]{1,0:T(8,128)(2,1)}, bf16[256,256]{1,0:T(8,128)(2,1)}, u32[]{:S(2)}, u32[]{:S(2)}) collective-permute-start(bf16[256,256]{1,0:T(8,128)(2,1)} %collective-permute-done.12), channel_id=1, source_target_pairs={{0,240},{16,0},{32,16},{48,32},{64,48},{80,64},{96,80},{112,96},{1... | collective-permute-start | bytes 393224 | tf_op jit(solution)/shard_map/ppermute | solution.py:28
  51.9 5.9 %collective-permute-start.7 = (bf16[256,256]{1,0:T(8,128)(2,1)}, bf16[256,256]{1,0:T(8,128)(2,1)}, u32[]{:S(2)}, u32[]{:S(2)}) collective-permute-start(bf16[256,256]{1,0:T(8,128)(2,1)} %collective-permute-done.6), channel_id=1, source_target_pairs={{0,16},{16,32},{32,48},{48,64},{64,80},{80,96},{96,112},{112,128},... | collective-permute-start | bytes 393224 | tf_op jit(solution)/shard_map/ppermute | solution.py:24
  54.7 11.6 %collective-permute-start.14 = (bf16[256,256]{1,0:T(8,128)(2,1)}, bf16[256,256]{1,0:T(8,128)(2,1)S(1)}, u32[]{:S(2)}, u32[]{:S(2)}) collective-permute-start(bf16[256,256]{1,0:T(8,128)(2,1)} %collective-permute-done.13), channel_id=1, source_target_pairs={{0,240},{16,0},{32,16},{48,32},{64,48},{80,64},{96,80},{112,96},{1... | collective-permute-start | bytes 393224 | tf_op jit(solution)/shard_map/ppermute | solution.py:28
  120.1 256.5 %reduce-scatter.3.cloned.1.call-start = ((), (), s32[]{:S(2)}) async-start(), calls=%async_computation.4 | async-start | bytes 2228224 | tf_op jit(solution)/shard_map/reduce_scatter | solution.py:134
  124.4 169.8 %copy-start.3 = (f32[512,512]{0,1:T(8,128)S(1)}, f32[512,512]{0,1:T(8,128)}, u32[]{:S(2)}) copy-start(f32[512,512]{0,1:T(8,128)} %copy-done.2) | copy-start | bytes 3145732
  (21 other events, 194.1 us)
Sparse Core Ops, SparseCore 0:
  10.4 54.6 all-gather.4
  66.9 39.1 all-gather.2
  120.2 173.9 reduce-scatter.4
  298.2 78.3 reduce-scatter.2
